TPU v7x, 32 devices: a whole 2x2x4 slice. The times are simulated.
32 devices in a mesh: groups: 2 (over y), col: 4 (over z), aux: 2 (over x), rep: 2 (over core).
Axes of the slice: x: 2, y: 2, z: 4, core: 2. Of those that a mesh axis runs over, the one named last changes fastest.
Arguments:
- b_aux: bfloat16 [4, 4096, 2400], P(('groups', 'aux'), ('col', 'rep')), parts along dimension 0, may hold values from -0.59765625 to 0.59765625
- occ_energies: float32 [2], P('groups'), parts along dimension 0, may hold values from -2 to -0.3
- vir_energies: float32 [4800], P('groups'), parts along dimension 0, may hold values from 0.2 to 3
- owners: int32 [2], replicated, may hold values from 0 to 7
Outputs:
- gamma: float32 [4, 4096, 2400], P(('groups', 'aux'), None, ('col', 'rep')), parts along dimension 0
There are 2 independent parts, one for each index of `groups`. A program takes and returns all parts, laid end to end along the dimension named above; an argument that names none is the same for every part. Nothing has to cross between parts.
Inputs may be any that keep to these rules, and one draw needn't show every extreme that they name: owners[s] is a column shard index in the order of col+rep; owners may repeat.
All inputs are finite; a program needn't handle non-finite values.
Results may differ from a plain program's by a relative error of at most 0.003.
Values may be sent and summed in bfloat16 or wider, within the bound.
No kernel may reach another device: no remote copies, remote signals or barrier semaphores. Data moves between devices by JAX's collectives and lax.ppermute only.
A program may use at most 64 MiB of HBM per device.

v0:
```python
import jax
import jax.numpy as jnp
from jax import lax
from jax.sharding import PartitionSpec as P

os_scale = 1.3


def from_root(value, axis, source):
    kept = jnp.where(lax.axis_index(axis) == source, value, 0).astype(value.dtype)
    return lax.psum(kept, axis)


def column_energy(first, occ_energies, vir_energies, width):
    nvirt = vir_energies.shape[0]
    occ_value = lax.dynamic_index_in_dim(occ_energies, first // nvirt, 0, keepdims=False)
    vir_values = lax.dynamic_slice_in_dim(vir_energies, first % nvirt, width, 0)
    return vir_values - occ_value


def body(b_aux, occ_energies, vir_energies, owners):
    moved = lax.all_to_all(b_aux, ("col", "rep"), split_axis=2, concat_axis=1, tiled=True)
    local_cols = moved[0]
    width = local_cols.shape[1]
    shard_index = lax.axis_index(("col", "rep"))
    energy_mine = column_energy(shard_index * width, occ_energies, vir_energies, width)
    gamma_acc = jnp.zeros(local_cols.shape, jnp.float32)
    for step_index in range(owners.shape[0]):
        owner_shard = owners[step_index]
        owner_cols = from_root(local_cols, ("col", "rep"), owner_shard)
        owner_energy = column_energy(owner_shard * width, occ_energies, vir_energies, width)
        denominator = energy_mine[:, None] + owner_energy[None, :]
        partial_value = lax.dot_general(
            local_cols, owner_cols, (((0,), (0,)), ((), ())), preferred_element_type=jnp.float32
        )
        coupling = lax.psum(partial_value, "aux")
        amplitude = (os_scale * coupling / denominator).astype(jnp.bfloat16)
        gamma_acc = gamma_acc + lax.dot_general(
            owner_cols, amplitude, (((1,), (1,)), ((), ())), preferred_element_type=jnp.float32
        )
    return gamma_acc[None]


def solution(mesh):
    placed = (P(("groups", "aux"), ("col", "rep"), None), P("groups"), P("groups"), P())
    return jax.shard_map(
        body,
        mesh=mesh,
        in_specs=placed,
        out_specs=P(("groups", "aux"), None, ("col", "rep")),
        check_vma=False,
    )
```

profile of v0, /device:TPU:0, one launch (start us, length us, event | category | flops | bytes accessed | tf_op | source)
XLA Modules:
  0.0 311.1 jit_solution(7487857900732730221)
XLA Ops:
  6.5 13.4 %copy.16 = bf16[1,512,2400]{1,0,2:T(2,128)(2,1)} copy(bf16[1,512,2400]{1,2,0:T(8,128)(2,1)} %param.4) | data formatting | bytes 4915200 | tf_op args[0]
  20.0 0.6 broadcast.16
  20.6 16.3 %reduce.2 = bf16[2400,512]{1,0:T(8,128)(2,1)S(1)} reduce(bf16[2400,1,512]{2,1,0:T(2,128)(2,1)} %bitcast.32, bf16[]{:T(256)} %broadcast.16), dimensions={1}, to_apply=%bitcast.30.reduce_sub_computation | reduce | bytes 4915202
  36.9 2.4 reshape.5
  39.3 0.0 copy-start.4
  39.3 6.5 %all-to-all-start = ((bf16[8,2,76800]{2,1,0:T(2,128)(2,1)}), bf16[8,2,76800]{2,1,0:T(2,128)(2,1)S(1)}, u32[]{:S(2)}, u32[]{:S(2)}) async-start(bf16[8,2,76800]{2,1,0:T(2,128)(2,1)} %reshape.5), calls=%async_computation | async-start | bytes 4915200 | tf_op jit(solution)/shard_map/all_to_all | solution.py:22
  45.7 0.0 all-reduce.7.cloned.1.call-start
  45.8 0.0 copy-done.4
  45.8 0.6 fusion.10
  47.7 54.8 %all-to-all-done = bf16[8,2,76800]{2,1,0:T(2,128)(2,1)S(1)} async-done(((bf16[8,2,76800]{2,1,0:T(2,128)(2,1)}), bf16[8,2,76800]{2,1,0:T(2,128)(2,1)S(1)}, u32[]{:S(2)}, u32[]{:S(2)}) %all-to-all-start) | async-done | bytes 2457632 | tf_op jit(solution)/shard_map/all_to_all | solution.py:22
  102.5 4.4 %reshape.6 = bf16[2400,1,512]{2,1,0:T(2,128)(2,1)} reshape(bf16[8,2,76800]{2,1,0:T(2,128)(2,1)S(1)} %all-to-all-done) | data formatting | bytes 4915200
  107.0 17.2 %bitcast_reduce_fusion = bf16[512,2400]{0,1:T(8,128)(2,1)} fusion(bf16[2400,1,512]{2,1,0:T(2,128)(2,1)} %reshape.6), kind=kLoop, calls=%fused_computation.22 | loop fusion | bytes 4915200 | tf_op jit(solution)/shard_map/all_to_all | solution.py:22
  124.1 2.6 all_to_all.12
  126.8 1.4 copy.15
  128.1 0.2 pad
  128.3 1.1 copy.12
  129.4 2.6 broadcast_select_fusion
  132.1 0.0 all-reduce.7.cloned.1.call-update
  132.1 0.2 all-reduce.5.cloned.1.call-start
  132.3 110.6 %all-reduce.7.cloned.1.call-done = (bf16[4096,300]{0,1:T(8,128)(2,1)}, bf16[4096,300]{0,1:T(8,128)(2,1)}) async-done(((bf16[4096,300]{0,1:T(8,128)(2,1)}, bf16[4096,300]{0,1:T(8,128)(2,1)}), (bf16[4096,300]{0,1:T(8,128)(2,1)}, bf16[4096,300]{0,1:T(8,128)(2,1)})) %all-reduce.7.cloned.1.call-update) | async-done | bytes 4915216 | tf_op jit(solution)/shard_map/psum | solution.py:11
  242.9 0.0 copy-start
  242.9 4.1 %convolution_bitcast_fusion.1 = f32[300,300]{0,1:T(8,128)} fusion(bf16[4096,300]{0,1:T(8,128)(2,1)} %get-tuple-element.7, bf16[4096,300]{0,1:T(8,128)(2,1)S(1)} %bitcast.34), kind=kOutput, calls=%fused_computation.6 | convolution fusion | flops 737280000 | bytes 5275200 | tf_op jit(solution)/shard_map/dot_general | solution.py:33
  247.0 0.0 copy-done
  247.0 0.0 copy-start.3
  247.0 2.3 convolution_bitcast_fusion
  249.2 0.0 all-reduce.5.cloned.1.call-update
  251.2 0.0 copy-done.3
  251.2 0.1 dynamic-slice_subtract_fusion
  251.3 35.9 %all-reduce.5.cloned.1.call-done = (f32[300,300]{0,1:T(8,128)}, f32[300,300]{0,1:T(8,128)}) async-done(((f32[300,300]{0,1:T(8,128)}, f32[300,300]{0,1:T(8,128)}), (f32[300,300]{0,1:T(8,128)}, f32[300,300]{0,1:T(8,128)})) %all-reduce.5.cloned.1.call-update) | async-done | bytes 720016 | tf_op jit(solution)/shard_map/psum | solution.py:36
  287.2 0.0 copy-start.1
  287.2 0.0 copy-start.2
  287.2 3.5 %fusion.1 = f32[4096,300]{0,1:T(8,128)S(1)} fusion(bf16[4096,300]{0,1:T(8,128)(2,1)} %get-tuple-element.7, f32[300,300]{0,1:T(8,128)} %get-tuple-element.5, f32[300]{0:T(512)S(1)} %get-tuple-element.13, f32[300]{0:T(512)S(1)} %get-tuple-element.12), kind=kOutput, calls=%fused_computation.9 | convolution fusion | flops 737640000 | bytes 7735200 | tf_op jit(solution)/shard_map/dot_general | solution.py:38
  290.7 0.0 copy-done.1
  290.7 0.0 copy-done.2
  290.7 3.9 %fusion = f32[1,4096,300]{1,2,0:T(8,128)} fusion(f32[4096,300]{0,1:T(8,128)S(1)} %fusion.1, bf16[4096,300]{0,1:T(8,128)(2,1)S(1)} %copy-done.1, f32[300,300]{0,1:T(8,128)S(1)} %copy-done.2, f32[300]{0:T(512)S(1)} %get-tuple-element.11, f32[300]{0:T(512)S(1)} %get-tuple-element.12), kind=kOutput, calls=%fused_computation.1 | convolution fusion | flops 738868800 | bytes 12650400 | tf_op jit(solution)/shard_map/dot_general | solution.py:38
  294.6 9.7 %copy.10 = f32[1,4096,300]{1,0,2:T(1,128)} copy(f32[1,4096,300]{1,2,0:T(8,128)} %fusion) | data formatting | bytes 9830400 | tf_op jit(solution)/shard_map/broadcast_in_dim | solution.py:41
Async XLA Ops:
  39.3 6.5 %copy-start.4 = (s32[2]{0:T(128)S(1)}, s32[2]{0:T(128)}, u32[]{:S(2)}) copy-start(s32[2]{0:T(128)} %param.7) | copy-start | bytes 28
  39.3 63.2 %all-to-all-start = ((bf16[8,2,76800]{2,1,0:T(2,128)(2,1)}), bf16[8,2,76800]{2,1,0:T(2,128)(2,1)S(1)}, u32[]{:S(2)}, u32[]{:S(2)}) async-start(bf16[8,2,76800]{2,1,0:T(2,128)(2,1)} %reshape.5), calls=%async_computation | async-start | bytes 4915200 | tf_op jit(solution)/shard_map/all_to_all | solution.py:22
  45.7 197.1 %all-reduce.7.cloned.1.call-start = ((), (), s32[]{:S(2)}) async-start(), calls=%async_computation.2 | async-start | bytes 9961472 | tf_op jit(solution)/shard_map/psum | solution.py:11
  132.1 155.1 %all-reduce.5.cloned.1.call-start = ((), (), s32[]{:S(2)}) async-start(), calls=%async_computation.1 | async-start | bytes 1867776 | tf_op jit(solution)/shard_map/psum | solution.py:36
  242.9 4.1 %copy-start = (bf16[4096,300]{0,1:T(8,128)(2,1)S(1)}, bf16[4096,300]{0,1:T(8,128)(2,1)}, u32[]{:S(2)}) copy-start(bf16[4096,300]{0,1:T(8,128)(2,1)} %get-tuple-element.8) | copy-start | bytes 7372804
  247.0 4.2 %copy-start.3 = (f32[2400]{0:T(1024)S(1)}, f32[2400]{0:T(1024)}, u32[]{:S(2)}) copy-start(f32[2400]{0:T(1024)} %param.6) | copy-start | bytes 28804
  287.2 3.5 %copy-start.1 = (bf16[4096,300]{0,1:T(8,128)(2,1)S(1)}, bf16[4096,300]{0,1:T(8,128)(2,1)}, u32[]{:S(2)}) copy-start(bf16[4096,300]{0,1:T(8,128)(2,1)} %get-tuple-element.8) | copy-start | bytes 7372804
  287.2 3.5 %copy-start.2 = (f32[300,300]{0,1:T(8,128)S(1)}, f32[300,300]{0,1:T(8,128)}, u32[]{:S(2)}) copy-start(f32[300,300]{0,1:T(8,128)} %get-tuple-element.6) | copy-start | bytes 1080004
Sparse Core Ops, SparseCore 0:
  132.2 110.6 all-reduce.6
  249.4 37.7 all-reduce.4
where the time goes:
time: 312 us; the launch traced here: 311 us
  waiting for transfers between devices  201 us (64%)
  local copies, waits for them, and re-layouts  53.6 us (17%)
  other arithmetic  19.1 us (6%)
  between operations  16.7 us (5%)
  matrix products  13.7 us (4%)
  starting transfers between devices  6.72 us (2%)
    psum x1, waiting for transfers between devices, from_root(): return lax.psum(kept, axis)  111 us
    all_to_all x1, waiting for transfers between devices, body(): lax.all_to_all(b_aux, ('col', 'rep'), split_axis=2, concat_axis=1, tiled=...  54.8 us
    psum x1, waiting for transfers between devices, body(): coupling = lax.psum(partial_value, 'aux')  35.9 us
    unnamed x16, local copies, waits for them, and re-layouts  22.1 us
    all_to_all x3, local copies, waits for them, and re-layouts, body(): lax.all_to_all(b_aux, ('col', 'rep'), split_axis=2, concat_axis=1, tiled=...  21.1 us
    unnamed x1, other arithmetic  16.3 us
    broadcast_in_dim x1, local copies, waits for them, and re-layouts, body(): return gamma_acc[None]  9.71 us
    dot_general x2, matrix products, body(): lax.dot_general(owner_cols, amplitude, (((1,), (1,)), ((), ())), preferre...  7.4 us
  transfers between devices with their start and end apart: 3, of which 3 were waited for; matrix products, arithmetic and copies ran while one was open for 0% of the time, Pallas kernels for 0%

commit v1 on v0

--- a/solution.py
+++ b/solution.py
@@ -33,7 +33,7 @@
         partial_value = lax.dot_general(
             local_cols, owner_cols, (((0,), (0,)), ((), ())), preferred_element_type=jnp.float32
         )
-        coupling = lax.psum(partial_value, "aux")
+        coupling = jnp.sum(lax.all_gather(partial_value, "aux"), axis=0)
         amplitude = (os_scale * coupling / denominator).astype(jnp.bfloat16)
         gamma_acc = gamma_acc + lax.dot_general(
             owner_cols, amplitude, (((1,), (1,)), ((), ())), preferred_element_type=jnp.float32

time: 312 us -> 301 us (0.965)
  waiting for transfers between devices: 201 us -> 163 us
  blocking collectives: 0 us -> 25.6 us
  local copies, waits for them, and re-layouts: 53.6 us -> 56.9 us
    psum x1 -> x0, waiting for transfers between devices: 35.9 us -> none  [body(): coupling = lax.psum(partial_value, 'aux')]
    all_gather x0 -> x2, blocking collectives: none -> 25.6 us  [body(): coupling = jnp.sum(lax.all_gather(partial_value, 'aux'), axis=0)]
    unnamed x16 -> x20, local copies, waits for them, and re-layouts: 22.1 us -> 25.5 us
  transfers between devices with their start and end apart: 3 -> 2, of which waited for: 3 -> 2; matrix products, arithmetic and copies ran while one was open for 0% -> 0% of each run, Pallas kernels for 0% -> 0%
where the time goes in v1:
time: 301 us
  waiting for transfers between devices  163 us (54%)
  local copies, waits for them, and re-layouts  56.9 us (19%)
  blocking collectives  25.6 us (9%)
  other arithmetic  19.9 us (7%)
  between operations  16.7 us (6%)
  matrix products  11.4 us (4%)
  starting transfers between devices  6.67 us (2%)
    psum x1, waiting for transfers between devices, from_root(): return lax.psum(kept, axis)  109 us
    all_to_all x1, waiting for transfers between devices, body(): lax.all_to_all(b_aux, ('col', 'rep'), split_axis=2, concat_axis=1, tiled=...  54.7 us
    all_gather x2, blocking collectives, body(): coupling = jnp.sum(lax.all_gather(partial_value, 'aux'), axis=0)  25.6 us
    unnamed x20, local copies, waits for them, and re-layouts  25.5 us
    all_to_all x3, local copies, waits for them, and re-layouts, body(): lax.all_to_all(b_aux, ('col', 'rep'), split_axis=2, concat_axis=1, tiled=...  21.1 us
    unnamed x1, other arithmetic  16.2 us
    broadcast_in_dim x1, local copies, waits for them, and re-layouts, body(): return gamma_acc[None]  9.71 us
    dot_general x2, matrix products, body(): lax.dot_general(owner_cols, amplitude, (((1,), (1,)), ((), ())), preferre...  6.65 us
  transfers between devices with their start and end apart: 2, of which 2 were waited for; matrix products, arithmetic and copies ran while one was open for 0% of the time, Pallas kernels for 0%

profile of v1, /device:TPU:0, one launch (start us, length us, event | category | flops | bytes accessed | tf_op | source)
XLA Modules:
  0.0 300.7 jit_solution(13206882089399694322)
XLA Ops:
  6.5 13.4 %copy.22 = bf16[1,512,2400]{1,0,2:T(2,128)(2,1)} copy(bf16[1,512,2400]{1,2,0:T(8,128)(2,1)} %param.4) | data formatting | bytes 4915200 | tf_op args[0]
  20.0 0.5 broadcast.16
  20.5 16.2 %reduce.4 = bf16[2400,512]{1,0:T(8,128)(2,1)S(1)} reduce(bf16[2400,1,512]{2,1,0:T(2,128)(2,1)} %bitcast.36, bf16[]{:T(256)} %broadcast.16), dimensions={1}, to_apply=%bitcast.34.reduce_sub_computation | reduce | bytes 4915202
  36.7 2.4 reshape.13
  39.1 0.0 copy-start.4
  39.1 6.5 %all-to-all-start = ((bf16[8,2,76800]{2,1,0:T(2,128)(2,1)}), bf16[8,2,76800]{2,1,0:T(2,128)(2,1)S(1)}, u32[]{:S(2)}, u32[]{:S(2)}) async-start(bf16[8,2,76800]{2,1,0:T(2,128)(2,1)} %reshape.13), calls=%async_computation | async-start | bytes 4915200 | tf_op jit(solution)/shard_map/all_to_all | solution.py:22
  45.5 0.2 all-reduce.3.cloned.1.call-start
  45.8 0.0 copy-done.4
  45.8 0.6 fusion.10
  47.6 54.7 %all-to-all-done = bf16[8,2,76800]{2,1,0:T(2,128)(2,1)S(1)} async-done(((bf16[8,2,76800]{2,1,0:T(2,128)(2,1)}), bf16[8,2,76800]{2,1,0:T(2,128)(2,1)S(1)}, u32[]{:S(2)}, u32[]{:S(2)}) %all-to-all-start) | async-done | bytes 2457632 | tf_op jit(solution)/shard_map/all_to_all | solution.py:22
  102.3 4.4 %reshape.14 = bf16[2400,1,512]{2,1,0:T(2,128)(2,1)} reshape(bf16[8,2,76800]{2,1,0:T(2,128)(2,1)S(1)} %all-to-all-done) | data formatting | bytes 4915200
  106.8 17.1 %bitcast_reduce_fusion = bf16[512,2400]{0,1:T(8,128)(2,1)} fusion(bf16[2400,1,512]{2,1,0:T(2,128)(2,1)} %reshape.14), kind=kLoop, calls=%fused_computation.22 | loop fusion | bytes 4915200 | tf_op jit(solution)/shard_map/all_to_all | solution.py:22
  123.9 2.6 all_to_all.12
  126.5 1.4 copy.21
  127.9 0.2 pad
  128.1 1.1 copy.18
  129.2 2.6 broadcast_select_fusion
  131.8 0.0 copy-start.3
  131.8 0.0 all-reduce.3.cloned.1.call-update
  133.8 0.0 copy-done.3
  133.8 0.1 dynamic-slice_subtract_fusion
  133.9 108.7 %all-reduce.3.cloned.1.call-done = (bf16[4096,300]{0,1:T(8,128)(2,1)}, bf16[4096,300]{0,1:T(8,128)(2,1)}) async-done(((bf16[4096,300]{0,1:T(8,128)(2,1)}, bf16[4096,300]{0,1:T(8,128)(2,1)}), (bf16[4096,300]{0,1:T(8,128)(2,1)}, bf16[4096,300]{0,1:T(8,128)(2,1)})) %all-reduce.3.cloned.1.call-update) | async-done | bytes 4915216 | tf_op jit(solution)/shard_map/psum | solution.py:11
  242.6 0.0 copy-start
  242.6 3.3 %convolution_bitcast_fusion.1 = f32[1,300,300]{1,2,0:T(8,128)S(1)} fusion(bf16[4096,300]{0,1:T(8,128)(2,1)} %get-tuple-element.5, bf16[4096,300]{0,1:T(8,128)(2,1)S(1)} %bitcast.38), kind=kOutput, calls=%fused_computation.6 | convolution fusion | flops 737280000 | bytes 5275200 | tf_op jit(solution)/shard_map/dot_general | solution.py:33
  246.0 0.0 copy-done
  246.0 1.5 convolution_bitcast_fusion
  247.4 1.0 copy.12
  248.4 0.2 copy.10
  248.6 13.0 %all-gather.2 = f32[2,300,300]{2,1,0:T(8,128)S(1)} all-gather(f32[1,300,300]{2,1,0:T(8,128)S(1)} %copy.10), channel_id=2, replica_groups=mesh['groups'=2,'col'=4,'aux'=2,'rep'=2] {'aux'}, dimensions={0}, use_global_device_ids=true | all-gather | bytes 1080000 | tf_op jit(solution)/shard_map/all_gather | solution.py:36
  261.7 0.1 reduce_sum.18
  261.8 0.0 copy-start.2
  261.8 1.0 copy.16
  262.8 12.6 %all-gather.3 = f32[2,300,300]{2,1,0:T(8,128)S(1)} all-gather(f32[1,300,300]{2,1,0:T(8,128)} %copy.12), channel_id=3, replica_groups=mesh['groups'=2,'col'=4,'aux'=2,'rep'=2] {'aux'}, dimensions={0}, use_global_device_ids=true | all-gather | bytes 1080000 | tf_op jit(solution)/shard_map/all_gather | solution.py:36
  275.3 0.9 reduce_sum.19
  276.2 1.2 copy.17
  277.4 0.0 copy-done.2
  277.4 0.0 copy-start.1
  277.4 2.8 fusion.1
  280.2 0.0 copy-done.1
  280.2 3.9 %fusion = f32[1,4096,300]{1,2,0:T(8,128)} fusion(f32[4096,300]{0,1:T(8,128)S(1)} %fusion.1, bf16[4096,300]{0,1:T(8,128)(2,1)S(1)} %copy-done.1, f32[300,300]{0,1:T(8,128)S(1)} %copy.17, f32[300]{0:T(512)S(1)} %get-tuple-element.9, f32[300]{0:T(512)S(1)} %get-tuple-element.10), kind=kOutput, calls=%fused_computation.1 | convolution fusion | flops 738868800 | bytes 12650400 | tf_op jit(solution)/shard_map/dot_general | solution.py:38
  284.1 9.7 %copy.14 = f32[1,4096,300]{1,0,2:T(1,128)} copy(f32[1,4096,300]{1,2,0:T(8,128)} %fusion) | data formatting | bytes 9830400 | tf_op jit(solution)/shard_map/broadcast_in_dim | solution.py:41
Async XLA Ops:
  39.1 6.7 %copy-start.4 = (s32[2]{0:T(128)S(1)}, s32[2]{0:T(128)}, u32[]{:S(2)}) copy-start(s32[2]{0:T(128)} %param.7) | copy-start | bytes 28
  39.1 63.2 %all-to-all-start = ((bf16[8,2,76800]{2,1,0:T(2,128)(2,1)}), bf16[8,2,76800]{2,1,0:T(2,128)(2,1)S(1)}, u32[]{:S(2)}, u32[]{:S(2)}) async-start(bf16[8,2,76800]{2,1,0:T(2,128)(2,1)} %reshape.13), calls=%async_computation | async-start | bytes 4915200 | tf_op jit(solution)/shard_map/all_to_all | solution.py:22
  45.5 197.1 %all-reduce.3.cloned.1.call-start = ((), (), s32[]{:S(2)}) async-start(), calls=%async_computation.1 | async-start | bytes 9961472 | tf_op jit(solution)/shard_map/psum | solution.py:11
  131.8 2.0 copy-start.3
  242.6 3.3 %copy-start = (bf16[4096,300]{0,1:T(8,128)(2,1)S(1)}, bf16[4096,300]{0,1:T(8,128)(2,1)}, u32[]{:S(2)}) copy-start(bf16[4096,300]{0,1:T(8,128)(2,1)} %get-tuple-element.6) | copy-start | bytes 7372804
  261.8 15.7 %copy-start.2 = (bf16[4096,300]{0,1:T(8,128)(2,1)S(1)}, bf16[4096,300]{0,1:T(8,128)(2,1)}, u32[]{:S(2)}) copy-start(bf16[4096,300]{0,1:T(8,128)(2,1)} %get-tuple-element.5) | copy-start | bytes 7372804
  277.4 2.8 copy-start.1
Sparse Core Ops, SparseCore 0:
  132.0 110.6 all-reduce.2
